TPU v7x, 256 devices: a whole 4x4x8 slice. The times are simulated.
256 devices in a mesh: dp: 32 (over x, z_hi, core), tensor: 8 (over y, z_lo).
Axes of the slice: x: 4, y: 4, z: 8 (z_hi: 4, z_lo: 2; z = z_hi * 2 + z_lo), core: 2. Of those that a mesh axis runs over, the one named last changes fastest.
Arguments:
- stream: bfloat16 [64, 430, 2048], P('dp', None, 'tensor'), may hold values from -3 to 3
- normed: bfloat16 [64, 430, 2048], P('dp'), may hold values from -6 to 6
- query_weight: bfloat16 [2048, 2048], P(None, 'tensor'), as said below
- key_weight: bfloat16 [2048, 2048], P(None, 'tensor'), as said below
- value_weight: bfloat16 [2048, 2048], P(None, 'tensor'), may hold values from -0.125 to 0.125
- out_weight: bfloat16 [2048, 2048], P('tensor'), may hold values from -0.125 to 0.125
- norm_gain: bfloat16 [2048], P('tensor'), may hold values from 0.099609375 to 1.8984375
- proj_weight: bfloat16 [2048, 1024], P('tensor'), may hold values from -0.125 to 0.125
- images: bfloat16 [64, 1024], P('dp'), may hold values from -6 to 6
Outputs:
- mean_loss: float32 [], replicated
- grad_normed: bfloat16 [64, 430, 2048], P('dp', None, 'tensor')
- grad_query: float32 [2048, 2048], P('dp', 'tensor')
- grad_key: float32 [2048, 2048], P('dp', 'tensor')
- grad_value: float32 [2048, 2048], P('dp', 'tensor')
- grad_out: float32 [2048, 2048], P('tensor', 'dp')
- grad_proj: float32 [2048, 1024], P('tensor', 'dp')
Inputs may be any that keep to these rules, and one draw needn't show every extreme that they name: `query_weight`: query projection entries, independent draws of order 2048^-0.5. `key_weight`: key projection entries, of order 2048^-0.5, in some heads up to about sixteen times that, possibly aligned with the query projection.
All inputs are finite; a program needn't handle non-finite values.
Results may differ from a plain program's by a relative error of at most 0.02.
Values may be sent and summed in bfloat16 or wider, within the bound.
No kernel may reach another device: no remote copies, remote signals or barrier semaphores. Data moves between devices by JAX's collectives and lax.ppermute only.
A program may use at most 128 MiB of HBM per device.

v0:
```python
import jax
import jax.numpy as jnp
from jax import lax
from jax.sharding import PartitionSpec as P

D = 2048
H = 16


SCALE_LOGIT = 14.0
GRAD_SCALE = 256.0
EPSILON = 1e-05
HIGH = lax.Precision.HIGHEST


def project(inputs, weight):
    return jnp.einsum("bld,dc->blc", inputs, weight, preferred_element_type=jnp.float32).astype(
        jnp.bfloat16
    )


def split_heads(values, head_size):
    return values.reshape(values.shape[0], values.shape[1], values.shape[2] // head_size, head_size)


def chunks_rows(grad, parts):
    rows, cols = grad.shape
    return grad.reshape(parts, (rows // parts) * cols)


def chunks_cols(grad, parts):
    rows, cols = grad.shape
    return grad.reshape(rows, parts, cols // parts).transpose(1, 0, 2).reshape(parts, -1)


def xor_pairs(count, bit):
    return [(i, i ^ bit) for i in range(count)]


def tree_sum(value, axis, count):
    bit = 1
    while bit < count:
        value = value + lax.ppermute(value, axis, xor_pairs(count, bit))
        bit *= 2
    return value


def tree_gather(value, axis, count, dim):
    index = lax.axis_index(axis)
    bit = 1
    while bit < count:
        other = lax.ppermute(value, axis, xor_pairs(count, bit))
        low = (index // bit) % 2 == 0
        value = jnp.where(
            low,
            jnp.concatenate([value, other], dim),
            jnp.concatenate([other, value], dim),
        )
        bit *= 2
    return value


def tree_scatter(buffer, axis, count, order):
    index = lax.axis_index(axis)
    width = buffer.shape[1]
    levels = len(order)
    cube = buffer.reshape((2,) * levels + (width,))
    natural = [count // (2 ** (k + 1)) for k in range(levels)]
    cube = cube.transpose([natural.index(bit) for bit in order] + [levels])
    buffer = cube.reshape(count, width)
    for bit in order:
        rows = buffer.shape[0]
        halves = buffer.reshape(2, rows // 2, width)
        own = (index // bit) % 2
        keep = lax.dynamic_index_in_dim(halves, own, axis=0, keepdims=False)
        send = lax.dynamic_index_in_dim(halves, 1 - own, axis=0, keepdims=False)
        received = lax.ppermute(send.astype(jnp.bfloat16), axis, xor_pairs(count, bit))
        buffer = keep.astype(jnp.float32) + received.astype(jnp.float32)
    return buffer


def halving_order(count):
    bits = [2 ** k for k in range(count.bit_length() - 1)]
    if count == 32:
        return [1, 8, 2, 16, 4]
    return bits


def local(
    stream,
    normed,
    query_weight,
    key_weight,
    value_weight,
    out_weight,
    norm_gain,
    proj_weight,
    images,
):
    seq_count = normed.shape[0]
    length = normed.shape[1]
    col_count = query_weight.shape[1]
    feat_share = stream.shape[2]
    head_size = D // H
    scale_head = head_size ** (-0.5)
    dp_parts = lax.psum(1, "dp")
    t_parts = lax.psum(1, "tensor")
    t_index = lax.axis_index("tensor")
    gain_full = tree_gather(norm_gain, "tensor", t_parts, 0).astype(jnp.float32)
    gathered = tree_gather(images, "dp", dp_parts, 0).astype(jnp.float32)
    image_unit = gathered / jnp.sqrt(jnp.sum(gathered * gathered, axis=-1, keepdims=True) + EPSILON)

    queries = split_heads(project(normed, query_weight), head_size)
    keys_all = split_heads(project(normed, key_weight), head_size)
    values_all = split_heads(project(normed, value_weight), head_size)
    scores = (
        jnp.einsum("bqhd,bkhd->bhqk", queries, keys_all, preferred_element_type=jnp.float32)
        * scale_head
    )
    row_max = jnp.max(scores, axis=-1, keepdims=True)
    exp_scores = jnp.exp(scores - row_max)
    attn_prob = exp_scores / jnp.sum(exp_scores, axis=-1, keepdims=True)
    attn_half = attn_prob.astype(jnp.bfloat16)
    heads_out = jnp.einsum(
        "bhqk,bkhd->bqhd", attn_half, values_all, preferred_element_type=jnp.float32
    )
    head_concat = heads_out.astype(jnp.bfloat16).reshape(seq_count, length, col_count)
    partial_value = jnp.einsum(
        "blc,cd->bld", head_concat, out_weight, preferred_element_type=jnp.float32
    )
    blocks = (
        partial_value.astype(jnp.bfloat16)
        .reshape(seq_count, length, t_parts, feat_share)
        .transpose(2, 0, 1, 3)
    )
    arrived = lax.all_to_all(blocks, "tensor", 0, 0, tiled=True)
    own_residual = stream.astype(jnp.float32) + jnp.sum(arrived.astype(jnp.float32), axis=0)
    spread = jnp.broadcast_to(
        own_residual.astype(jnp.bfloat16)[None], (t_parts,) + own_residual.shape
    )
    collected = lax.all_to_all(spread, "tensor", 0, 0, tiled=True)
    residual = (
        collected.transpose(1, 2, 0, 3).reshape(seq_count, length, t_parts * feat_share)
    ).astype(jnp.float32)
    center = jnp.mean(residual, axis=-1, keepdims=True)
    offset = residual - center
    variance = jnp.mean(offset * offset, axis=-1, keepdims=True)
    inv_std = lax.rsqrt(variance + EPSILON)
    normal_feat = offset * inv_std
    pooled_full = jnp.mean(normal_feat * gain_full, axis=1)
    pooled = lax.dynamic_slice_in_dim(pooled_full, t_index * feat_share, feat_share, 1).astype(
        jnp.bfloat16
    )
    embedded = tree_sum(
        jnp.dot(pooled, proj_weight, preferred_element_type=jnp.float32), "tensor", t_parts
    )
    embed_norm = jnp.sqrt(jnp.sum(embedded * embedded, axis=-1, keepdims=True) + EPSILON)
    spectra = embedded / embed_norm
    logits = SCALE_LOGIT * jnp.dot(spectra, image_unit.T, precision=HIGH)
    own_start = lax.axis_index("dp") * seq_count
    columns = jnp.arange(logits.shape[1], dtype=jnp.int32)
    own_rows = own_start + jnp.arange(seq_count, dtype=jnp.int32)
    matches = (columns[None, :] == own_rows[:, None]).astype(jnp.float32)
    exp_logits = jnp.exp(logits)
    row_lse = jnp.log(jnp.sum(exp_logits, axis=1))
    diagonal = jnp.sum(logits * matches, axis=1)
    local_loss = 0.5 * jnp.sum(row_lse) - jnp.sum(diagonal)
    loss_terms = tree_sum(
        jnp.concatenate([jnp.sum(exp_logits, axis=0), local_loss[None]]), "dp", dp_parts
    )
    col_total = loss_terms[:-1]
    loss_sum = loss_terms[-1]
    col_lse = jnp.log(col_total)
    mean_loss = (loss_sum + 0.5 * jnp.sum(col_lse)) / logits.shape[1]
    grad_logits = GRAD_SCALE * (
        0.5 * jnp.exp(logits - row_lse[:, None])
        + 0.5 * jnp.exp(logits - col_lse[None, :])
        - matches
    )
    grad_spec = SCALE_LOGIT * jnp.dot(grad_logits, image_unit, precision=HIGH)
    radial = jnp.sum(spectra * grad_spec, axis=-1, keepdims=True)
    grad_embed = ((grad_spec - spectra * radial) / embed_norm).astype(jnp.bfloat16)
    grad_proj = lax.dot_general(
        pooled, grad_embed, (((0,), (0,)), ((), ())), preferred_element_type=jnp.float32
    )
    grad_pooled = lax.dot_general(
        grad_embed, proj_weight, (((1,), (1,)), ((), ())), preferred_element_type=jnp.float32
    )
    grad_pooled_full = tree_gather(grad_pooled, "tensor", t_parts, 1)
    grad_normal = jnp.broadcast_to(
        grad_pooled_full[:, None, :] / length, normal_feat.shape
    ) * gain_full
    mean_one = jnp.mean(grad_normal, axis=-1, keepdims=True)
    mean_two = jnp.mean(grad_normal * normal_feat, axis=-1, keepdims=True)
    piece_rows = (inv_std * (grad_normal - mean_one - normal_feat * mean_two)).astype(jnp.bfloat16)
    grad_heads = jnp.einsum(
        "blw,cw->blc", piece_rows, out_weight, preferred_element_type=jnp.float32
    )
    grad_out = jnp.einsum("blc,blw->cw", head_concat, piece_rows, preferred_element_type=jnp.float32)
    grad_heads = split_heads(grad_heads.astype(jnp.bfloat16), head_size)
    grad_probs = jnp.einsum(
        "bqhd,bkhd->bhqk", grad_heads, values_all, preferred_element_type=jnp.float32
    )
    row_dot = jnp.sum(attn_prob * grad_probs, axis=-1, keepdims=True)
    grad_scores = (attn_prob * (grad_probs - row_dot) * scale_head).astype(jnp.bfloat16)
    grad_q = (
        jnp.einsum("bhqk,bkhd->bqhd", grad_scores, keys_all, preferred_element_type=jnp.float32)
        .astype(jnp.bfloat16)
        .reshape(seq_count, length, col_count)
    )
    grad_k = (
        jnp.einsum("bhqk,bqhd->bkhd", grad_scores, queries, preferred_element_type=jnp.float32)
        .astype(jnp.bfloat16)
        .reshape(seq_count, length, col_count)
    )
    grad_v = (
        jnp.einsum("bhqk,bqhd->bkhd", attn_half, grad_heads, preferred_element_type=jnp.float32)
        .astype(jnp.bfloat16)
        .reshape(seq_count, length, col_count)
    )
    back_input = jnp.einsum("blc,dc->bld", grad_q, query_weight, preferred_element_type=jnp.float32)
    back_input = back_input + jnp.einsum(
        "blc,dc->bld", grad_k, key_weight, preferred_element_type=jnp.float32
    )
    back_input = back_input + jnp.einsum(
        "blc,dc->bld", grad_v, value_weight, preferred_element_type=jnp.float32
    )
    late_pieces = [
        chunks_cols(grad_out.astype(jnp.bfloat16), dp_parts),
        chunks_cols(grad_proj.astype(jnp.bfloat16), dp_parts),
    ]
    late_reduced = tree_scatter(jnp.concatenate(late_pieces, axis=1), "dp", dp_parts, halving_order(dp_parts))
    grad_query = jnp.einsum("bld,blc->dc", normed, grad_q, preferred_element_type=jnp.float32)
    grad_key = jnp.einsum("bld,blc->dc", normed, grad_k, preferred_element_type=jnp.float32)
    grad_value = jnp.einsum("bld,blc->dc", normed, grad_v, preferred_element_type=jnp.float32)
    early_pieces = [
        chunks_rows(grad_query.astype(jnp.bfloat16), dp_parts),
        chunks_rows(grad_key.astype(jnp.bfloat16), dp_parts),
        chunks_rows(grad_value.astype(jnp.bfloat16), dp_parts),
    ]
    back_half, early_joined = lax.optimization_barrier(
        (back_input.astype(jnp.bfloat16), jnp.concatenate(early_pieces, axis=1))
    )
    grad_normed = lax.psum_scatter(back_half, "tensor", scatter_dimension=2, tiled=True)
    early_reduced = tree_scatter(early_joined, "dp", dp_parts, halving_order(dp_parts))
    widths = [piece.shape[1] for piece in early_pieces + late_pieces]
    reduced = jnp.concatenate([early_reduced, late_reduced], axis=1)
    outs = []
    start = 0
    for width in widths:
        outs.append(reduced[0, start:start + width])
        start += width
    rows_q = D // dp_parts
    grad_query_out = outs[0].reshape(rows_q, col_count)
    grad_key_out = outs[1].reshape(rows_q, col_count)
    grad_value_out = outs[2].reshape(rows_q, col_count)
    grad_out_out = outs[3].reshape(grad_out.shape[0], grad_out.shape[1] // dp_parts)
    grad_proj_out = outs[4].reshape(grad_proj.shape[0], grad_proj.shape[1] // dp_parts)
    return (
        mean_loss,
        grad_normed,
        grad_query_out,
        grad_key_out,
        grad_value_out,
        grad_out_out,
        grad_proj_out,
    )


def solution(mesh):
    return jax.shard_map(
        local,
        mesh=mesh,
        in_specs=(
            P("dp", None, "tensor"),
            P("dp", None, None),
            P(None, "tensor"),
            P(None, "tensor"),
            P(None, "tensor"),
            P("tensor", None),
            P("tensor"),
            P("tensor", None),
            P("dp", None),
        ),
        out_specs=(
            P(),
            P("dp", None, "tensor"),
            P("dp", "tensor"),
            P("dp", "tensor"),
            P("dp", "tensor"),
            P("tensor", "dp"),
            P("tensor", "dp"),
        ),
        check_vma=False,
    )
```

profile of v0, /device:TPU:1, one launch (start us, length us, event | category | flops | bytes accessed | tf_op | source)
XLA Modules:
  0.0 508.4 jit_solution(191865921743435397)
XLA Ops:
  7.2 4.5 fusion.57
  11.8 4.2 fusion.60
  16.9 2.8 fusion.146
  23.9 4.8 fusion.63
  29.4 2.8 convolution_convert_fusion
  32.2 4.7 reshape.353
  36.9 4.7 copy.312
  41.6 47.9 %all_to_all.10 = bf16[8,2,430,256]{3,1,2,0:T(2,128)(2,1)S(1)} all-to-all(bf16[8,2,430,256]{3,1,2,0:T(2,128)(2,1)S(1)} %copy.312), channel_id=1, replica_groups=mesh['dp'=32,'tensor'=8] {'tensor'}, dimensions={0} | all-to-all | bytes 7045120 | tf_op jit(solution)/shard_map/all_to_all | solution.py:136
  92.4 3.6 broadcast_in_dim.8
  96.0 4.6 all-to-all-start.1
  105.4 3.1 collective-permute-start.7
  108.5 31.5 %collective-permute-done = bf16[256]{0:T(256)(128)(2,1)S(1)} collective-permute-done((bf16[256]{0:T(256)(128)(2,1)S(1)}, bf16[256]{0:T(256)(128)(2,1)S(1)}, u32[]{:S(2)}, u32[]{:S(2)}) %collective-permute-start) | collective-permute-done | bytes 544 | tf_op jit(solution)/shard_map/ppermute | solution.py:52
  140.4 6.1 %collective-permute-start.8 = (bf16[8,1024]{1,0:T(8,128)(2,1)S(1)}, bf16[8,1024]{1,0:T(8,128)(2,1)S(1)}, u32[]{:S(2)}, u32[]{:S(2)}) collective-permute-start(bf16[8,1024]{1,0:T(8,128)(2,1)S(1)} %maximum_select_fusion.3), channel_id=1, source_target_pairs={{0,32},{8,40},{16,48},{24,56},{32,0},{40,8},{48,16},{56,24},{64,96... | collective-permute-start | bytes 49160 | tf_op jit(solution)/shard_map/ppermute | solution.py:52
  146.5 11.3 %collective-permute-start.2 = (bf16[1024]{0:T(1024)(128)(2,1)S(1)}, bf16[1024]{0:T(1024)(128)(2,1)S(1)}, u32[]{:S(2)}, u32[]{:S(2)}) collective-permute-start(bf16[1024]{0:T(1024)(128)(2,1)S(1)} %maximum_select_fusion.11), channel_id=1, source_target_pairs={{0,4},{1,5},{2,6},{3,7},{4,0},{5,1},{6,2},{7,3},{8,12},{9,13},{10,... | collective-permute-start | bytes 6152 | tf_op jit(solution)/shard_map/ppermute | solution.py:52
  163.6 4.9 fusion.9
  168.7 6.8 %multiply_reduce_fusion.2 = f32[2,430]{0,1:T(8,128)S(1)} fusion(bf16[8,2,430,256]{3,1,2,0:T(2,128)(2,1)} %all-to-all-done.1, f32[2,430]{0,1:T(8,128)S(1)} %copy.316), kind=kLoop, calls=%fused_computation.15 | loop fusion | flops 7044260 | bytes 3529440 | tf_op jit(solution)/shard_map/reduce_sum | solution.py:147
  175.9 7.8 %multiply_reduce_fusion.1 = f32[2,8,256]{2,0,1:T(2,128)S(1)} fusion(bf16[8,2,430,256]{3,1,2,0:T(2,128)(2,1)} %all-to-all-done.1, f32[8,256]{1,0:T(8,128)S(1)} %reshape.370, f32[2,430]{0,1:T(8,128)S(1)} %copy.318, f32[2,430]{0,1:T(8,128)S(1)} %copy.316), kind=kLoop, calls=%fused_computation.14 | loop fusion | flops 8802304 | bytes 3554016 | tf_op jit(solution)/shard_map/reduce_sum | solution.py:150
  190.2 2.9 collective-permute-done.5
  196.2 8.6 %collective-permute-start.11 = (f32[65]{0:T(128)S(1)}, f32[65]{0:T(128)S(1)}, u32[]{:S(2)}, u32[]{:S(2)}) collective-permute-start(f32[65]{0:T(128)S(1)} %pad_maximum_fusion.1), channel_id=1, source_target_pairs={{0,8},{8,0},{16,24},{24,16},{32,40},{40,32},{48,56},{56,48},{64,72... | collective-permute-start | bytes 788 | tf_op jit(solution)/shard_map/ppermute | solution.py:43
  211.6 3.8 collective-permute-done.13
  218.2 3.5 collective-permute-done.15
  223.8 7.3 %convert_bitcast_fusion = f32[2,430,8,256]{3,0,1,2:T(2,128)} fusion(bf16[8,2,430,256]{3,1,2,0:T(2,128)(2,1)} %all-to-all-done.1), kind=kLoop, calls=%fused_computation.13 | loop fusion | flops 1761280 | bytes 10567680 | tf_op jit(solution)/shard_map/convert_element_type | solution.py:144
  231.1 7.3 %copy.320 = f32[2,430,8,256]{3,2,1,0:T(8,128)} copy(f32[2,430,8,256]{3,0,1,2:T(2,128)} %convert_bitcast_fusion) | data formatting | bytes 14090240 | tf_op jit(solution)/shard_map/convert_element_type | solution.py:144
  238.4 5.4 %reshape.371 = f32[2,430,2048]{2,1,0:T(8,128)} reshape(f32[2,430,8,256]{3,2,1,0:T(8,128)} %copy.320) | data formatting | bytes 14090240 | tf_op jit(solution)/shard_map/convert_element_type | solution.py:144
  256.3 8.6 %fusion.5 = f32[2,430]{0,1:T(8,128)S(1)} fusion(bf16[8,2,430,256]{3,1,2,0:T(2,128)(2,1)} %all-to-all-done.1, f32[2,8,256]{2,0,1:T(2,128)S(1)} %bitcast.153, f32[8,256]{1,0:T(8,128)S(1)} %reshape.370, f32[2,430]{0,1:T(8,128)} %copy-done.9, f32[2,430]{0,1:T(8,128)S(1)} %copy.316), kind=kLoop, calls=%fused_computation.10 | loop fusion | flops 10566820 | bytes 3557456 | tf_op jit(solution)/shard_map/reduce_sum | solution.py:194
  265.1 4.8 fusion.45
  270.1 5.2 %fusion.64 = bf16[2,430,2,128]{3,1,2,0:T(8,128)(2,1)} fusion(bf16[2,430,2,128]{3,2,1,0:T(2,128)(2,1)S(1)} %reshape.354, f32[2,2,430]{2,1,0:T(2,128)S(1)} %get-tuple-element.90, f32[2,2,430,430]{2,3,1,0:T(8,128)} %copy-done.3), kind=kOutput, calls=%fused_computation.75 | convolution fusion | flops 193257904 | bytes 3845920 | tf_op jit(solution)/shard_map/bhqk,bqhd->bkhd/dot_general | solution.py:217
  277.7 7.4 %fusion.65 = bf16[2,430,2,128]{3,1,2,0:T(8,128)(2,1)} fusion(f32[2,2,430,430]{2,3,1,0:T(8,128)} %fusion.87, bf16[2,430,2,128]{3,2,1,0:T(2,128)(2,1)S(1)} %copy-done.12, f32[2,2,430,430]{2,3,1,0:T(8,128)} %get-tuple-element.91, f32[2,2,430]{2,1,0:T(2,128)S(1)} %get-tuple-element.90), kind=kOutput, calls=%fused_computation.76 | convolution fusion | flops 194737104 | bytes 6804320 | tf_op jit(solution)/shard_map/bhqk,bqhd->bkhd/dot_general | solution.py:212
  285.1 7.7 %fusion.68 = bf16[2,430,2,128]{3,1,2,0:T(8,128)(2,1)} fusion(f32[2,2,430,430]{2,3,1,0:T(8,128)} %fusion.87, bf16[2,430,2,128]{3,2,1,0:T(2,128)(2,1)S(1)} %copy-done.14, f32[2,2,430,430]{2,3,1,0:T(8,128)} %get-tuple-element.91, f32[2,2,430]{2,1,0:T(2,128)S(1)} %get-tuple-element.90), kind=kOutput, calls=%fused_computation.77 | convolution fusion | flops 194737104 | bytes 6804320 | tf_op jit(solution)/shard_map/bhqk,bkhd->bqhd/dot_general | solution.py:207
  292.8 9.9 %fusion.8 = bf16[2,430,8,256]{3,0,1,2:T(2,128)(2,1)S(1)} fusion(bf16[8,2,430,256]{3,1,2,0:T(2,128)(2,1)} %all-to-all-done.1, f32[2,430]{0,1:T(8,128)S(1)} %copy.340, f32[2,430]{0,1:T(8,128)S(1)} %copy.339, f32[2,8,256]{2,0,1:T(2,128)S(1)} %bitcast.154, f32[8,256]{1,0:T(8,128)S(1)} %reshape.370, f32[2,430]{0,1:T(8,128)S(1)} %copy-done.10, f32[2,430]{0,1:T(8,128)S(1)} %copy.316), kind=kLoop, calls=%fused_computation.17 | loop fusion | flops 15851520 | bytes 7083456 | tf_op jit(solution)/shard_map/convert_element_type | solution.py:195
  304.9 4.4 convert_element_type.271
  309.3 3.3 fusion.22
  321.6 3.4 constant_dynamic-slice_fusion
  326.8 6.4 %collective-permute-start.24 = (bf16[16,24576]{1,0:T(8,128)(2,1)}, bf16[16,24576]{1,0:T(8,128)(2,1)}, u32[]{:S(2)}, u32[]{:S(2)}) collective-permute-start(bf16[16,24576]{1,0:T(8,128)(2,1)} %bitcast.145), channel_id=1, source_target_pairs={{0,8},{8,0},{16,24},{24,16},{32,40},{40,32},{48,56},{56,48},{64,72... | collective-permute-start | bytes 2359304 | tf_op jit(solution)/shard_map/ppermute | solution.py:77
  333.8 4.5 fusion.23
  343.0 4.4 fusion.24
  353.5 4.6 fusion.25
  361.0 3.1 pad_maximum_fusion
  370.0 3.0 add_convert_fusion
  373.0 5.1 %reshape.361 = bf16[2,2,2,2,2,49152]{5,4,3,2,1,0:T(2,128)(2,1)} reshape(bf16[32,49152]{1,0:T(8,128)(2,1)} %pad_maximum_fusion) | data formatting | bytes 6291456 | tf_op jit(solution)/shard_map/reshape | solution.py:67
  378.1 6.0 %copy.338 = bf16[2,2,2,2,2,49152]{5,0,4,3,2,1:T(2,128)(2,1)} copy(bf16[2,2,2,2,2,49152]{5,0,2,4,1,3:T(2,128)(2,1)} %bitcast.149) | data formatting | bytes 6291456 | tf_op jit(solution)/shard_map/transpose | solution.py:69
  386.0 11.1 %constant_dynamic-slice_fusion.1 = (bf16[1,16,49152]{2,0,1:T(2,128)(2,1)S(1)}, f32[1,16,49152]{2,0,1:T(1,128)}) fusion(bf16[2,16,49152]{2,0,1:T(2,128)(2,1)} %bitcast.146, s32[]{:T(128)S(6)} %select_n.328, s32[]{:T(128)S(6)} %select_n.327), kind=kLoop, calls=%fused_computation.155 | loop fusion | flops 786432 | bytes 7864328 | tf_op jit(solution)/shard_map/jit(dynamic_index_in_dim)/dynamic_slice | solution.py:76
  402.6 4.2 fusion.13
  408.5 17.5 %collective-permute-done.20 = bf16[8,49152]{1,0:T(8,128)(2,1)S(1)} collective-permute-done((bf16[8,49152]{1,0:T(8,128)(2,1)S(1)}, bf16[8,49152]{1,0:T(8,128)(2,1)S(1)}, u32[]{:S(2)}, u32[]{:S(2)}) %collective-permute-start.20) | collective-permute-done | bytes 786464 | tf_op jit(solution)/shard_map/ppermute | solution.py:77
  432.9 16.5 %collective-permute-done.21 = bf16[4,49152]{1,0:T(4,128)(2,1)S(1)} collective-permute-done((bf16[4,49152]{1,0:T(4,128)(2,1)S(1)}, bf16[4,49152]{1,0:T(4,128)(2,1)S(1)}, u32[]{:S(2)}, u32[]{:S(2)}) %collective-permute-start.21) | collective-permute-done | bytes 393248 | tf_op jit(solution)/shard_map/ppermute | solution.py:77
  453.4 3.4 collective-permute-done.28
  461.8 12.3 %collective-permute-done.23 = bf16[1,49152]{1,0:T(2,128)(2,1)S(1)} collective-permute-done((bf16[1,49152]{1,0:T(2,128)(2,1)S(1)}, bf16[1,49152]{1,0:T(2,128)(2,1)S(1)}, u32[]{:S(2)}, u32[]{:S(2)}) %collective-permute-start.23) | collective-permute-done | bytes 98336 | tf_op jit(solution)/shard_map/ppermute | solution.py:77
  477.9 20.2 %reduce-scatter.2.cloned.1.call-done = bf16[2,430,256]{2,1,0:T(8,128)(2,1)} async-done(((bf16[2,430,2048]{2,1,0:T(8,128)(2,1)}), bf16[2,430,256]{2,1,0:T(8,128)(2,1)}) %reduce-scatter.2.cloned.1.call-update) | async-done | bytes 440336 | tf_op jit(solution)/shard_map/reduce_scatter | solution.py:244
  (224 shorter events, 117.9 us)
Async XLA Ops:
  7.2 22.2 %copy-start = (bf16[256,2048]{1,0:T(8,128)(2,1)S(1)}, bf16[256,2048]{1,0:T(8,128)(2,1)}, u32[]{:S(2)}) copy-start(bf16[256,2048]{1,0:T(8,128)(2,1)} %param.14) | copy-start | bytes 3145732
  7.2 4.6 copy-start.17
  16.8 4.6 copy-start.2
  16.9 4.8 copy-start.20
  23.9 4.9 copy-start.15
  29.4 7.5 %copy-start.6 = (bf16[2,430,256]{2,1,0:T(8,128)(2,1)}, bf16[2,430,256]{2,1,0:T(8,128)(2,1)S(1)}, u32[]{:S(2)}) copy-start(bf16[2,430,256]{2,1,0:T(8,128)(2,1)S(1)} %reshape.352) | copy-start | bytes 1320964
  96.0 4.7 copy-start.27
  96.0 6.1 %copy-start.26 = (bf16[2,1024]{1,0:T(2,128)(2,1)S(1)}, bf16[2,1024]{1,0:T(2,128)(2,1)}, u32[]{:S(2)}) copy-start(bf16[2,1024]{1,0:T(2,128)(2,1)} %param.17) | copy-start | bytes 12292
  96.0 67.6 %all-to-all-start.1 = ((bf16[8,2,430,256]{3,1,2,0:T(2,128)(2,1)}), bf16[8,2,430,256]{3,1,2,0:T(2,128)(2,1)}, u32[]{:S(2)}, u32[]{:S(2)}) async-start(bf16[8,2,430,256]{3,1,2,0:T(2,128)(2,1)} %broadcast_in_dim.8), calls=%async_computation.1 | async-start | bytes 7045120 | tf_op jit(solution)/shard_map/all_to_all | solution.py:141
  100.6 397.4 %reduce-scatter.2.cloned.1.call-start = ((), (), s32[]{:S(2)}) async-start(), calls=%async_computation.3 | async-start | bytes 3981312 | tf_op jit(solution)/shard_map/reduce_scatter | solution.py:244
  100.7 39.3 %collective-permute-start = (bf16[256]{0:T(256)(128)(2,1)S(1)}, bf16[256]{0:T(256)(128)(2,1)S(1)}, u32[]{:S(2)}, u32[]{:S(2)}) collective-permute-start(bf16[256]{0:T(256)(128)(2,1)S(1)} %copy-done.27), channel_id=1, source_target_pairs={{0,1},{1,0},{2,3},{3,2},{4,5},{5,4},{6,7},{7,6},{8,9},{9,8},{10,11... | collective-permute-start | bytes 1544 | tf_op jit(solution)/shard_map/ppermute | solution.py:52
  102.1 3.3 collective-permute-start.6
  105.4 35.0 %collective-permute-start.7 = (bf16[4,1024]{1,0:T(4,128)(2,1)S(1)}, bf16[4,1024]{1,0:T(4,128)(2,1)S(1)}, u32[]{:S(2)}, u32[]{:S(2)}) collective-permute-start(bf16[4,1024]{1,0:T(4,128)(2,1)S(1)} %maximum_select_fusion.6), channel_id=1, source_target_pairs={{0,16},{8,24},{16,0},{24,8},{32,48},{40,56},{48,32},{56,40},{64,80... | collective-permute-start | bytes 24584 | tf_op jit(solution)/shard_map/ppermute | solution.py:52
  140.0 6.5 %collective-permute-start.1 = (bf16[512]{0:T(512)(128)(2,1)S(1)}, bf16[512]{0:T(512)(128)(2,1)S(1)}, u32[]{:S(2)}, u32[]{:S(2)}) collective-permute-start(bf16[512]{0:T(512)(128)(2,1)S(1)} %maximum_select_fusion.12), channel_id=1, source_target_pairs={{0,2},{1,3},{2,0},{3,1},{4,6},{5,7},{6,4},{7,5},{8,10},{9,11},{10,... | collective-permute-start | bytes 3080 | tf_op jit(solution)/shard_map/ppermute | solution.py:52
  140.4 17.5 %collective-permute-start.8 = (bf16[8,1024]{1,0:T(8,128)(2,1)S(1)}, bf16[8,1024]{1,0:T(8,128)(2,1)S(1)}, u32[]{:S(2)}, u32[]{:S(2)}) collective-permute-start(bf16[8,1024]{1,0:T(8,128)(2,1)S(1)} %maximum_select_fusion.3), channel_id=1, source_target_pairs={{0,32},{8,40},{16,48},{24,56},{32,0},{40,8},{48,16},{56,24},{64,96... | collective-permute-start | bytes 49160 | tf_op jit(solution)/shard_map/ppermute | solution.py:52
  146.5 12.9 %collective-permute-start.2 = (bf16[1024]{0:T(1024)(128)(2,1)S(1)}, bf16[1024]{0:T(1024)(128)(2,1)S(1)}, u32[]{:S(2)}, u32[]{:S(2)}) collective-permute-start(bf16[1024]{0:T(1024)(128)(2,1)S(1)} %maximum_select_fusion.11), channel_id=1, source_target_pairs={{0,4},{1,5},{2,6},{3,7},{4,0},{5,1},{6,2},{7,3},{8,12},{9,13},{10,... | collective-permute-start | bytes 6152 | tf_op jit(solution)/shard_map/ppermute | solution.py:52
  157.9 2.9 collective-permute-start.9
  160.8 26.2 %collective-permute-start.10 = (bf16[32,1024]{1,0:T(8,128)(2,1)S(1)}, bf16[32,1024]{1,0:T(8,128)(2,1)S(1)}, u32[]{:S(2)}, u32[]{:S(2)}) collective-permute-start(bf16[32,1024]{1,0:T(8,128)(2,1)S(1)} %maximum_select_fusion.1), channel_id=1, source_target_pairs={{0,128},{8,136},{16,144},{24,152},{32,160},{40,168},{48,176},{56,1... | collective-permute-start | bytes 196616 | tf_op jit(solution)/shard_map/ppermute | solution.py:52
  168.7 14.9 %copy-start.22 = (bf16[256,1024]{1,0:T(8,128)(2,1)S(1)}, bf16[256,1024]{1,0:T(8,128)(2,1)}, u32[]{:S(2)}) copy-start(bf16[256,1024]{1,0:T(8,128)(2,1)} %param.16) | copy-start | bytes 1572868
  175.8 46.9 %copy-start.9 = (f32[2,430]{0,1:T(8,128)}, f32[2,430]{0,1:T(8,128)S(1)}, u32[]{:S(2)}) copy-start(f32[2,430]{0,1:T(8,128)S(1)} %copy.318) | copy-start | bytes 10324
  183.9 2.5 collective-permute-start.3
  186.4 2.5 collective-permute-start.4
  188.9 4.2 collective-permute-start.5
  196.2 9.4 %collective-permute-start.11 = (f32[65]{0:T(128)S(1)}, f32[65]{0:T(128)S(1)}, u32[]{:S(2)}, u32[]{:S(2)}) collective-permute-start(f32[65]{0:T(128)S(1)} %pad_maximum_fusion.1), channel_id=1, source_target_pairs={{0,8},{8,0},{16,24},{24,16},{32,40},{40,32},{48,56},{56,48},{64,72... | collective-permute-start | bytes 788 | tf_op jit(solution)/shard_map/ppermute | solution.py:43
  205.7 3.3 collective-permute-start.12
  209.0 6.3 %collective-permute-start.13 = (f32[65]{0:T(128)S(1)}, f32[65]{0:T(128)S(1)}, u32[]{:S(2)}, u32[]{:S(2)}) collective-permute-start(f32[65]{0:T(128)S(1)} %add.237), channel_id=1, source_target_pairs={{0,32},{8,40},{16,48},{24,56},{32,0},{40,8},{48,16},{56,24},{64,96... | collective-permute-start | bytes 788 | tf_op jit(solution)/shard_map/ppermute | solution.py:43
  215.4 2.4 collective-permute-start.14
  217.8 3.9 collective-permute-start.15
  223.0 20.8 %collective-permute-start.16 = (f32[2,256]{1,0:T(2,128)S(1)}, f32[2,256]{1,0:T(2,128)S(1)}, u32[]{:S(2)}, u32[]{:S(2)}) collective-permute-start(f32[2,256]{1,0:T(2,128)S(1)} %fusion.135), channel_id=1, source_target_pairs={{0,1},{1,0},{2,3},{3,2},{4,5},{5,4},{6,7},{7,6},{8,9},{9,8},{10,11... | collective-permute-start | bytes 6152 | tf_op jit(solution)/shard_map/ppermute | solution.py:52
  243.8 7.9 %collective-permute-start.17 = (f32[2,512]{1,0:T(2,128)S(1)}, f32[2,512]{1,0:T(2,128)S(1)}, u32[]{:S(2)}, u32[]{:S(2)}) collective-permute-start(f32[2,512]{1,0:T(2,128)S(1)} %maximum_select_fusion.9), channel_id=1, source_target_pairs={{0,2},{1,3},{2,0},{3,1},{4,6},{5,7},{6,4},{7,5},{8,10},{9,11},{10,... | collective-permute-start | bytes 12296 | tf_op jit(solution)/shard_map/ppermute | solution.py:52
  251.8 4.1 collective-permute-start.18
  270.1 5.2 %copy-start.16 = (bf16[2,430,2,128]{3,2,1,0:T(2,128)(2,1)S(1)}, bf16[2,430,2,128]{3,2,1,0:T(2,128)(2,1)}, u32[]{:S(2)}) copy-start(bf16[2,430,2,128]{3,2,1,0:T(2,128)(2,1)} %copy-done.15) | copy-start | bytes 1320964
  277.7 7.4 %copy-start.14 = (bf16[2,430,2,128]{3,2,1,0:T(2,128)(2,1)S(1)}, bf16[2,430,2,128]{3,2,1,0:T(2,128)(2,1)}, u32[]{:S(2)}) copy-start(bf16[2,430,2,128]{3,2,1,0:T(2,128)(2,1)} %copy-done.13) | copy-start | bytes 1320964
  285.1 7.7 %copy-start.10 = (f32[2,430]{0,1:T(8,128)S(1)}, f32[2,430]{0,1:T(8,128)}, u32[]{:S(2)}) copy-start(f32[2,430]{0,1:T(8,128)} %copy-done.9) | copy-start | bytes 10324
  321.5 11.6 %copy-start.24 = (bf16[2,430,2,128]{3,1,2,0:T(8,128)(2,1)S(1)}, bf16[2,430,2,128]{3,1,2,0:T(8,128)(2,1)}, u32[]{:S(2)}) copy-start(bf16[2,430,2,128]{3,1,2,0:T(8,128)(2,1)} %fusion.64) | copy-start | bytes 1320964
  326.8 39.8 %collective-permute-start.24 = (bf16[16,24576]{1,0:T(8,128)(2,1)}, bf16[16,24576]{1,0:T(8,128)(2,1)}, u32[]{:S(2)}, u32[]{:S(2)}) collective-permute-start(bf16[16,24576]{1,0:T(8,128)(2,1)} %bitcast.145), channel_id=1, source_target_pairs={{0,8},{8,0},{16,24},{24,16},{32,40},{40,32},{48,56},{56,48},{64,72... | collective-permute-start | bytes 2359304 | tf_op jit(solution)/shard_map/ppermute | solution.py:77
  333.8 8.6 %copy-start.23 = (bf16[2,430,2,128]{3,1,2,0:T(8,128)(2,1)S(1)}, bf16[2,430,2,128]{3,1,2,0:T(8,128)(2,1)}, u32[]{:S(2)}) copy-start(bf16[2,430,2,128]{3,1,2,0:T(8,128)(2,1)} %fusion.65) | copy-start | bytes 1320964
  369.9 14.2 %collective-permute-start.25 = (bf16[8,24576]{1,0:T(8,128)(2,1)S(1)}, bf16[8,24576]{1,0:T(8,128)(2,1)S(1)}, u32[]{:S(2)}, u32[]{:S(2)}) collective-permute-start(bf16[8,24576]{1,0:T(8,128)(2,1)S(1)} %fusion.85), channel_id=1, source_target_pairs={{0,64},{8,72},{16,80},{24,88},{32,96},{40,104},{48,112},{56,120},{... | collective-permute-start | bytes 1179656 | tf_op jit(solution)/shard_map/ppermute | solution.py:77
  378.1 6.0 %copy-start.5 = (f32[2,8,24576]{2,1,0:T(8,128)S(1)}, f32[2,8,24576]{2,1,0:T(8,128)}, u32[]{:S(2)}) copy-start(f32[2,8,24576]{2,1,0:T(8,128)} %copy-done.4) | copy-start | bytes 4718596
  384.5 14.9 %collective-permute-start.26 = (bf16[4,24576]{1,0:T(4,128)(2,1)S(1)}, bf16[4,24576]{1,0:T(4,128)(2,1)S(1)}, u32[]{:S(2)}, u32[]{:S(2)}) collective-permute-start(bf16[4,24576]{1,0:T(4,128)(2,1)S(1)} %fusion.98), channel_id=1, source_target_pairs={{0,16},{8,24},{16,0},{24,8},{32,48},{40,56},{48,32},{56,40},{64,80... | collective-permute-start | bytes 589832 | tf_op jit(solution)/shard_map/ppermute | solution.py:77
  398.8 3.8 collective-permute-start.19
  400.0 8.5 %collective-permute-start.27 = (bf16[2,24576]{1,0:T(2,128)(2,1)S(1)}, bf16[2,24576]{1,0:T(2,128)(2,1)S(1)}, u32[]{:S(2)}, u32[]{:S(2)}) collective-permute-start(bf16[2,24576]{1,0:T(2,128)(2,1)S(1)} %fusion.101), channel_id=1, source_target_pairs={{0,128},{8,136},{16,144},{24,152},{32,160},{40,168},{48,176},{56,1... | collective-permute-start | bytes 294920 | tf_op jit(solution)/shard_map/ppermute | solution.py:77
  406.9 19.1 %collective-permute-start.20 = (bf16[8,49152]{1,0:T(8,128)(2,1)S(1)}, bf16[8,49152]{1,0:T(8,128)(2,1)S(1)}, u32[]{:S(2)}, u32[]{:S(2)}) collective-permute-start(bf16[8,49152]{1,0:T(8,128)(2,1)S(1)} %fusion.83), channel_id=1, source_target_pairs={{0,64},{8,72},{16,80},{24,88},{32,96},{40,104},{48,112},{56,120},{... | collective-permute-start | bytes 2359304 | tf_op jit(solution)/shard_map/ppermute | solution.py:77
  429.1 20.4 %collective-permute-start.21 = (bf16[4,49152]{1,0:T(4,128)(2,1)S(1)}, bf16[4,49152]{1,0:T(4,128)(2,1)S(1)}, u32[]{:S(2)}, u32[]{:S(2)}) collective-permute-start(bf16[4,49152]{1,0:T(4,128)(2,1)S(1)} %fusion.84), channel_id=1, source_target_pairs={{0,16},{8,24},{16,0},{24,8},{32,48},{40,56},{48,32},{56,40},{64,80... | collective-permute-start | bytes 1179656 | tf_op jit(solution)/shard_map/ppermute | solution.py:77
  430.4 26.3 %collective-permute-start.28 = (bf16[1,24576]{1,0:T(2,128)(2,1)S(1)}, bf16[1,24576]{1,0:T(2,128)(2,1)S(1)}, u32[]{:S(2)}, u32[]{:S(2)}) collective-permute-start(bf16[1,24576]{1,0:T(2,128)(2,1)S(1)} %dynamic-slice_convert_fusion.9), channel_id=1, source_target_pairs={{0,32},{8,40},{16,48},{24,56},{32,0},{40,8},{48,16},{56,24},{64,96... | collective-permute-start | bytes 147464 | tf_op jit(solution)/shard_map/ppermute | solution.py:77
  449.5 50.7 %copy-start.1 = (bf16[256,2048]{1,0:T(8,128)(2,1)S(1)}, bf16[256,2048]{1,0:T(8,128)(2,1)}, u32[]{:S(2)}) copy-start(bf16[256,2048]{1,0:T(8,128)(2,1)} %param.14) | copy-start | bytes 3145732
  451.7 6.5 %collective-permute-start.22 = (bf16[2,49152]{1,0:T(2,128)(2,1)S(1)}, bf16[2,49152]{1,0:T(2,128)(2,1)S(1)}, u32[]{:S(2)}, u32[]{:S(2)}) collective-permute-start(bf16[2,49152]{1,0:T(2,128)(2,1)S(1)} %fusion.97), channel_id=1, source_target_pairs={{0,128},{8,136},{16,144},{24,152},{32,160},{40,168},{48,176},{56,1... | collective-permute-start | bytes 589832 | tf_op jit(solution)/shard_map/ppermute | solution.py:77
  458.6 15.6 %collective-permute-start.23 = (bf16[1,49152]{1,0:T(2,128)(2,1)S(1)}, bf16[1,49152]{1,0:T(2,128)(2,1)S(1)}, u32[]{:S(2)}, u32[]{:S(2)}) collective-permute-start(bf16[1,49152]{1,0:T(2,128)(2,1)S(1)} %dynamic-slice_convert_fusion.8), channel_id=1, source_target_pairs={{0,32},{8,40},{16,48},{24,56},{32,0},{40,8},{48,16},{56,24},{64,96... | collective-permute-start | bytes 294920 | tf_op jit(solution)/shard_map/ppermute | solution.py:77
  (11 other events, 30.9 us)
Sparse Core Ops, SparseCore 0:
  399.6 98.4 reduce-scatter.1
where the time goes:
time: 516 us; the launch traced here: 508 us
  waiting for transfers between devices  127 us (25%)
  local copies, waits for them, and re-layouts  90.5 us (18%)
  other arithmetic  81.9 us (16%)
  starting transfers between devices  71.4 us (14%)
  matrix products  70.6 us (14%)
  blocking collectives  47.9 us (9%)
  between operations  18.8 us (4%)
    ppermute x10, waiting for transfers between devices, tree_scatter(): lax.ppermute(send.astype(jnp.bfloat16), axis, xor_pairs(count, bit))  51.8 us
    all_to_all x1, blocking collectives, local(): arrived = lax.all_to_all(blocks, 'tensor', 0, 0, tiled=True)  47.9 us
    ppermute x11, waiting for transfers between devices, tree_gather(): other = lax.ppermute(value, axis, xor_pairs(count, bit))  36.2 us
    ppermute x11, starting transfers between devices, tree_gather(): other = lax.ppermute(value, axis, xor_pairs(count, bit))  31.4 us
    reduce_scatter x1, waiting for transfers between devices, local(): lax.psum_scatter(back_half, 'tensor', scatter_dimension=2, tiled=True)  20.2 us
    ppermute x10, starting transfers between devices, tree_scatter(): lax.ppermute(send.astype(jnp.bfloat16), axis, xor_pairs(count, bit))  19.8 us
    ppermute x8, waiting for transfers between devices, tree_sum(): value = value + lax.ppermute(value, axis, xor_pairs(count, bit))  19 us
    ppermute x8, starting transfers between devices, tree_sum(): value = value + lax.ppermute(value, axis, xor_pairs(count, bit))  15.5 us
  transfers between devices with their start and end apart: 31, of which 20 were waited for; matrix products, arithmetic and copies ran while one was open for 24% of the time, Pallas kernels for 0%

commit v1 on v0

--- a/solution.py
+++ b/solution.py
@@ -80,10 +80,7 @@
 
 
 def halving_order(count):
-    bits = [2 ** k for k in range(count.bit_length() - 1)]
-    if count == 32:
-        return [1, 8, 2, 16, 4]
-    return bits
+    return [count // (2 ** (k + 1)) for k in range(count.bit_length() - 1)]
 
 
 def local(
@@ -128,20 +125,15 @@
     partial_value = jnp.einsum(
         "blc,cd->bld", head_concat, out_weight, preferred_element_type=jnp.float32
     )
-    blocks = (
-        partial_value.astype(jnp.bfloat16)
-        .reshape(seq_count, length, t_parts, feat_share)
-        .transpose(2, 0, 1, 3)
-    )
-    arrived = lax.all_to_all(blocks, "tensor", 0, 0, tiled=True)
-    own_residual = stream.astype(jnp.float32) + jnp.sum(arrived.astype(jnp.float32), axis=0)
+    blocks = partial_value.astype(jnp.bfloat16).reshape(seq_count, length, t_parts, feat_share)
+    arrived = lax.all_to_all(blocks, "tensor", 2, 2, tiled=True)
+    own_residual = stream.astype(jnp.float32) + jnp.sum(arrived.astype(jnp.float32), axis=2)
     spread = jnp.broadcast_to(
-        own_residual.astype(jnp.bfloat16)[None], (t_parts,) + own_residual.shape
-    )
-    collected = lax.all_to_all(spread, "tensor", 0, 0, tiled=True)
-    residual = (
-        collected.transpose(1, 2, 0, 3).reshape(seq_count, length, t_parts * feat_share)
-    ).astype(jnp.float32)
+        own_residual.astype(jnp.bfloat16)[:, :, None, :],
+        (seq_count, length, t_parts, feat_share),
+    )
+    collected = lax.all_to_all(spread, "tensor", 2, 2, tiled=True)
+    residual = collected.reshape(seq_count, length, t_parts * feat_share).astype(jnp.float32)
     center = jnp.mean(residual, axis=-1, keepdims=True)
     offset = residual - center
     variance = jnp.mean(offset * offset, axis=-1, keepdims=True)

time: 516 us -> 491 us (0.952)
  local copies, waits for them, and re-layouts: 90.5 us -> 65.8 us
  starting transfers between devices: 71.4 us -> 86.4 us
  other arithmetic: 81.9 us -> 67.4 us
    ppermute x10, starting transfers between devices: 19.8 us -> 34.6 us  [tree_scatter(): lax.ppermute(send.astype(jnp.bfloat16), axis, xor_pairs(count, bit))]
    dynamic_slice x2 -> x0, other arithmetic: 14.5 us -> none  [tree_scatter(): send = lax.dynamic_index_in_dim(halves, 1 - own, axis=0, keepdims=False)]
    reduce_scatter x1, waiting for transfers between devices: 20.2 us -> 6.28 us  [local(): lax.psum_scatter(back_half, 'tensor', scatter_dimension=2, tiled=True)]
    transpose x3 -> x0, local copies, waits for them, and re-layouts: 11.8 us -> none  [the longest x2 7.13 us: tree_scatter(): cube = cube.transpose([natural.index(bit) for bit in order] + [levels])]
    ppermute x10, waiting for transfers between devices: 51.8 us -> 63.1 us  [tree_scatter(): lax.ppermute(send.astype(jnp.bfloat16), axis, xor_pairs(count, bit))]
    convert_element_type x3 -> x2, local copies, waits for them, and re-layouts: 13.1 us -> 5.77 us  [the longest x1 5.43 us: local(): collected.reshape(seq_count, length, t_parts * feat_share)]
    reduce_sum x1, other arithmetic: 6.81 us -> 13.9 us  [local(): variance = jnp.mean(offset * offset, axis=-1, keepdims=True)]
    reduce_sum x1, other arithmetic: 8.55 us -> 14.5 us  [local(): mean_two = jnp.mean(grad_normal * normal_feat, axis=-1, keepdims=True)]
  transfers between devices with their start and end apart: 31 -> 31, of which waited for: 20 -> 21; matrix products, arithmetic and copies ran while one was open for 24% -> 18% of each run, Pallas kernels for 0% -> 0%
where the time goes in v1:
time: 491 us; the launch traced here: 481 us
  waiting for transfers between devices  125 us (25%)
  starting transfers between devices  86.4 us (18%)
  matrix products  70.3 us (14%)
  other arithmetic  67.4 us (14%)
  local copies, waits for them, and re-layouts  65.8 us (13%)
  blocking collectives  47.9 us (10%)
  between operations  19 us (4%)
    ppermute x10, waiting for transfers between devices, tree_scatter(): lax.ppermute(send.astype(jnp.bfloat16), axis, xor_pairs(count, bit))  63.1 us
    all_to_all x1, blocking collectives, local(): arrived = lax.all_to_all(blocks, 'tensor', 2, 2, tiled=True)  47.9 us
    ppermute x11, waiting for transfers between devices, tree_gather(): other = lax.ppermute(value, axis, xor_pairs(count, bit))  36.2 us
    ppermute x10, starting transfers between devices, tree_scatter(): lax.ppermute(send.astype(jnp.bfloat16), axis, xor_pairs(count, bit))  34.6 us
    ppermute x11, starting transfers between devices, tree_gather(): other = lax.ppermute(value, axis, xor_pairs(count, bit))  31.8 us
    ppermute x8, waiting for transfers between devices, tree_sum(): value = value + lax.ppermute(value, axis, xor_pairs(count, bit))  19.1 us
    ppermute x8, starting transfers between devices, tree_sum(): value = value + lax.ppermute(value, axis, xor_pairs(count, bit))  15.4 us
    reduce_sum x1, other arithmetic, local(): mean_two = jnp.mean(grad_normal * normal_feat, axis=-1, keepdims=True)  14.5 us
  transfers between devices with their start and end apart: 31, of which 21 were waited for; matrix products, arithmetic and copies ran while one was open for 18% of the time, Pallas kernels for 0%

profile of v1, /device:TPU:1, one launch (start us, length us, event | category | flops | bytes accessed | tf_op | source)
XLA Modules:
  0.0 481.4 jit_solution(15852807301187892794)
XLA Ops:
  7.2 4.5 fusion.56
  11.8 4.2 fusion.59
  16.9 2.8 fusion.145
  23.9 4.8 %fusion.62 = bf16[2,430,2,128]{3,1,2,0:T(8,128)(2,1)S(1)} fusion(bf16[2,430,2,128]{3,2,1,0:T(2,128)(2,1)S(1)} %reshape.345, f32[2,2,430]{2,1,0:T(2,128)S(1)} %get-tuple-element.72, f32[2,2,430,430]{2,3,1,0:T(8,128)} %copy-done.3), kind=kOutput, calls=%fused_computation.71 | convolution fusion | flops 193257904 | bytes 3845920 | tf_op jit(solution)/shard_map/bhqk,bkhd->bqhd/dot_general | solution.py:121
  29.4 2.8 convolution_convert_fusion
  32.2 4.7 reshape.349
  36.9 4.7 copy.237
  41.6 47.9 %all_to_all.10 = bf16[2,430,8,256]{3,0,1,2:T(2,128)(2,1)S(1)} all-to-all(bf16[2,430,8,256]{3,0,1,2:T(2,128)(2,1)S(1)} %copy.237), channel_id=1, replica_groups=mesh['dp'=32,'tensor'=8] {'tensor'}, dimensions={2} | all-to-all | bytes 7045120 | tf_op jit(solution)/shard_map/all_to_all | solution.py:129
  92.4 3.6 broadcast_in_dim.8
  96.0 4.6 all-to-all-start.1
  105.4 3.1 collective-permute-start.7
  108.5 31.5 %collective-permute-done = bf16[256]{0:T(256)(128)(2,1)S(1)} collective-permute-done((bf16[256]{0:T(256)(128)(2,1)S(1)}, bf16[256]{0:T(256)(128)(2,1)S(1)}, u32[]{:S(2)}, u32[]{:S(2)}) %collective-permute-start) | collective-permute-done | bytes 544 | tf_op jit(solution)/shard_map/ppermute | solution.py:52
  140.4 6.1 %collective-permute-start.8 = (bf16[8,1024]{1,0:T(8,128)(2,1)S(1)}, bf16[8,1024]{1,0:T(8,128)(2,1)S(1)}, u32[]{:S(2)}, u32[]{:S(2)}) collective-permute-start(bf16[8,1024]{1,0:T(8,128)(2,1)S(1)} %maximum_select_fusion.3), channel_id=1, source_target_pairs={{0,32},{8,40},{16,48},{24,56},{32,0},{40,8},{48,16},{56,24},{64,96... | collective-permute-start | bytes 49160 | tf_op jit(solution)/shard_map/ppermute | solution.py:52
  146.5 11.3 %collective-permute-start.2 = (bf16[1024]{0:T(1024)(128)(2,1)S(1)}, bf16[1024]{0:T(1024)(128)(2,1)S(1)}, u32[]{:S(2)}, u32[]{:S(2)}) collective-permute-start(bf16[1024]{0:T(1024)(128)(2,1)S(1)} %maximum_select_fusion.11), channel_id=1, source_target_pairs={{0,4},{1,5},{2,6},{3,7},{4,0},{5,1},{6,2},{7,3},{8,12},{9,13},{10,... | collective-permute-start | bytes 6152 | tf_op jit(solution)/shard_map/ppermute | solution.py:52
  160.7 2.8 collective-permute-start.10
  163.6 3.6 convert_reduce_fusion.1
  167.2 13.9 %multiply_reduce_fusion.2 = f32[2,430]{1,0:T(2,128)S(1)} fusion(f32[2,430]{1,0:T(2,128)S(1)} %broadcast_multiply_fusion.3, bf16[2,430,8,256]{3,0,1,2:T(2,128)(2,1)} %all-to-all-done.1), kind=kLoop, calls=%fused_computation.15 | loop fusion | flops 7044260 | bytes 3529440 | tf_op jit(solution)/shard_map/reduce_sum | solution.py:139
  181.2 4.7 multiply_reduce_fusion.1
  192.3 2.9 collective-permute-done.5
  198.2 8.6 %collective-permute-start.11 = (f32[65]{0:T(128)S(1)}, f32[65]{0:T(128)S(1)}, u32[]{:S(2)}, u32[]{:S(2)}) collective-permute-start(f32[65]{0:T(128)S(1)} %pad_maximum_fusion.1), channel_id=1, source_target_pairs={{0,8},{8,0},{16,24},{24,16},{32,40},{40,32},{48,56},{56,48},{64,72... | collective-permute-start | bytes 788 | tf_op jit(solution)/shard_map/ppermute | solution.py:43
  213.5 3.9 collective-permute-done.13
  220.5 3.5 collective-permute-done.15
  226.0 5.5 %copy_convert_fusion = f32[2,430,8,256]{3,2,1,0:T(8,128)} fusion(bf16[2,430,8,256]{3,0,1,2:T(2,128)(2,1)} %all-to-all-done.1), kind=kLoop, calls=%fused_computation.61 | loop fusion | flops 1761280 | bytes 10567680 | tf_op jit(solution)/shard_map/convert_element_type | solution.py:136
  231.5 5.4 %reshape.366 = f32[2,430,2048]{2,1,0:T(8,128)} reshape(f32[2,430,8,256]{3,2,1,0:T(8,128)} %copy_convert_fusion) | data formatting | bytes 14090240 | tf_op jit(solution)/shard_map/convert_element_type | solution.py:136
  240.9 3.0 concatenate.199
  250.0 14.5 %fusion.5 = f32[2,430]{1,0:T(2,128)S(1)} fusion(f32[2,8,256]{2,1,0:T(8,128)S(1)} %bitcast.132, f32[8,256]{1,0:T(8,128)S(1)} %reshape.365, f32[2,430]{1,0:T(2,128)S(1)} %add_rsqrt_fusion, f32[2,430]{1,0:T(2,128)S(1)} %broadcast_multiply_fusion.3, bf16[2,430,8,256]{3,0,1,2:T(2,128)(2,1)} %all-to-all-done.1), kind=kLoop, calls=%fused_computation.10 | loop fusion | flops 10566820 | bytes 3557456 | tf_op jit(solution)/shard_map/reduce_sum | solution.py:186
  264.5 4.8 fusion.44
  269.4 5.2 %fusion.63 = bf16[2,430,2,128]{3,1,2,0:T(8,128)(2,1)} fusion(bf16[2,430,2,128]{3,2,1,0:T(2,128)(2,1)S(1)} %reshape.350, f32[2,2,430]{2,1,0:T(2,128)S(1)} %get-tuple-element.72, f32[2,2,430,430]{2,3,1,0:T(8,128)} %copy-done.3), kind=kOutput, calls=%fused_computation.72 | convolution fusion | flops 193257904 | bytes 3845920 | tf_op jit(solution)/shard_map/bhqk,bqhd->bkhd/dot_general | solution.py:209
  277.0 7.4 %fusion.64 = bf16[2,430,2,128]{3,1,2,0:T(8,128)(2,1)} fusion(f32[2,2,430,430]{2,3,1,0:T(8,128)} %fusion.86, bf16[2,430,2,128]{3,2,1,0:T(2,128)(2,1)S(1)} %copy-done.15, f32[2,2,430,430]{2,3,1,0:T(8,128)} %get-tuple-element.73, f32[2,2,430]{2,1,0:T(2,128)S(1)} %get-tuple-element.72), kind=kOutput, calls=%fused_computation.73 | convolution fusion | flops 194737104 | bytes 6804320 | tf_op jit(solution)/shard_map/bhqk,bqhd->bkhd/dot_general | solution.py:204
  284.4 7.6 %fusion.67 = bf16[2,430,2,128]{3,1,2,0:T(8,128)(2,1)} fusion(f32[2,2,430,430]{2,3,1,0:T(8,128)} %fusion.86, bf16[2,430,2,128]{3,2,1,0:T(2,128)(2,1)S(1)} %copy-done.17, f32[2,2,430,430]{2,3,1,0:T(8,128)} %get-tuple-element.73, f32[2,2,430]{2,1,0:T(2,128)S(1)} %get-tuple-element.72), kind=kOutput, calls=%fused_computation.74 | convolution fusion | flops 194737104 | bytes 6804320 | tf_op jit(solution)/shard_map/bhqk,bkhd->bqhd/dot_general | solution.py:199
  292.0 9.1 %fusion.8 = bf16[2,430,8,256]{3,2,1,0:T(8,128)(2,1)} fusion(f32[2,430]{1,0:T(2,128)S(1)} %broadcast_multiply_fusion.1, f32[2,430]{1,0:T(2,128)S(1)} %broadcast_multiply_fusion.2, f32[2,8,256]{2,1,0:T(8,128)S(1)} %bitcast.133, f32[8,256]{1,0:T(8,128)S(1)} %reshape.365, f32[2,430]{1,0:T(2,128)S(1)} %add_rsqrt_fusion, ...), kind=kLoop, calls=%fused_computation.13 | loop fusion | flops 15851520 | bytes 7083456 | tf_op jit(solution)/shard_map/convert_element_type | solution.py:187
  301.1 4.4 convert_element_type.266
  305.5 3.3 fusion.21
  319.0 4.4 fusion.22
  326.9 4.4 fusion.23
  335.6 4.4 fusion.24
  341.1 2.9 pad_maximum_fusion
  349.3 2.9 add_convert_fusion
  352.2 2.8 collective-permute-done.25
  355.4 2.7 collective-permute-start.26
  368.0 22.4 %collective-permute-done.19 = bf16[16,49152]{1,0:T(8,128)(2,1)S(1)} collective-permute-done((bf16[16,49152]{1,0:T(8,128)(2,1)}, bf16[16,49152]{1,0:T(8,128)(2,1)S(1)}, u32[]{:S(2)}, u32[]{:S(2)}) %collective-permute-start.19) | collective-permute-done | bytes 1572896 | tf_op jit(solution)/shard_map/ppermute | solution.py:77
  393.1 13.8 %collective-permute-done.20 = bf16[8,49152]{1,0:T(8,128)(2,1)S(1)} collective-permute-done((bf16[8,49152]{1,0:T(8,128)(2,1)S(1)}, bf16[8,49152]{1,0:T(8,128)(2,1)S(1)}, u32[]{:S(2)}, u32[]{:S(2)}) %collective-permute-start.20) | collective-permute-done | bytes 786464 | tf_op jit(solution)/shard_map/ppermute | solution.py:77
  409.9 3.4 collective-permute-start.21
  413.4 9.7 %collective-permute-start.28 = (bf16[1,24576]{1,0:T(2,128)(2,1)S(1)}, bf16[1,24576]{1,0:T(2,128)(2,1)S(1)}, u32[]{:S(2)}, u32[]{:S(2)}) collective-permute-start(bf16[1,24576]{1,0:T(2,128)(2,1)S(1)} %dynamic-slice_convert_fusion.7), channel_id=1, source_target_pairs={{0,8},{8,0},{16,24},{24,16},{32,40},{40,32},{48,56},{56,48},{64,72... | collective-permute-start | bytes 147464 | tf_op jit(solution)/shard_map/ppermute | solution.py:77
  423.0 13.4 %collective-permute-done.21 = bf16[4,49152]{1,0:T(4,128)(2,1)S(1)} collective-permute-done((bf16[4,49152]{1,0:T(4,128)(2,1)S(1)}, bf16[4,49152]{1,0:T(4,128)(2,1)S(1)}, u32[]{:S(2)}, u32[]{:S(2)}) %collective-permute-start.21) | collective-permute-done | bytes 393248 | tf_op jit(solution)/shard_map/ppermute | solution.py:77
  441.0 8.2 %collective-permute-done.22 = bf16[2,49152]{1,0:T(2,128)(2,1)S(1)} collective-permute-done((bf16[2,49152]{1,0:T(2,128)(2,1)S(1)}, bf16[2,49152]{1,0:T(2,128)(2,1)S(1)}, u32[]{:S(2)}, u32[]{:S(2)}) %collective-permute-start.22) | collective-permute-done | bytes 196640 | tf_op jit(solution)/shard_map/ppermute | solution.py:77
  449.5 10.3 %collective-permute-start.23 = (bf16[1,49152]{1,0:T(2,128)(2,1)S(1)}, bf16[1,49152]{1,0:T(2,128)(2,1)S(1)}, u32[]{:S(2)}, u32[]{:S(2)}) collective-permute-start(bf16[1,49152]{1,0:T(2,128)(2,1)S(1)} %dynamic-slice_convert_fusion.6), channel_id=1, source_target_pairs={{0,8},{8,0},{16,24},{24,16},{32,40},{40,32},{48,56},{56,48},{64,72... | collective-permute-start | bytes 294920 | tf_op jit(solution)/shard_map/ppermute | solution.py:77
  464.7 6.3 %reduce-scatter.2.cloned.1.call-done = bf16[2,430,256]{2,1,0:T(8,128)(2,1)} async-done(((bf16[2,430,2048]{2,1,0:T(8,128)(2,1)}), bf16[2,430,256]{2,1,0:T(8,128)(2,1)}) %reduce-scatter.2.cloned.1.call-update) | async-done | bytes 440336 | tf_op jit(solution)/shard_map/reduce_scatter | solution.py:236
  (217 shorter events, 99.8 us)
Async XLA Ops:
  7.2 22.2 %copy-start = (bf16[256,2048]{1,0:T(8,128)(2,1)S(1)}, bf16[256,2048]{1,0:T(8,128)(2,1)}, u32[]{:S(2)}) copy-start(bf16[256,2048]{1,0:T(8,128)(2,1)} %param.14) | copy-start | bytes 3145732
  7.2 4.6 copy-start.20
  11.8 4.4 copy-start.14
  16.2 3.5 copy-start.16
  16.8 3.6 copy-start.3
  16.8 4.6 copy-start.2
  16.9 4.8 %copy-start.23 = (bf16[2048,256]{1,0:T(8,128)(2,1)S(1)}, bf16[2048,256]{1,0:T(8,128)(2,1)}, u32[]{:S(2)}) copy-start(bf16[2048,256]{1,0:T(8,128)(2,1)} %param.13) | copy-start | bytes 3145732
  23.9 4.9 %copy-start.18 = (bf16[2,430,2,128]{3,2,1,0:T(2,128)(2,1)}, bf16[2,430,2,128]{3,2,1,0:T(2,128)(2,1)S(1)}, u32[]{:S(2)}) copy-start(bf16[2,430,2,128]{3,2,1,0:T(2,128)(2,1)S(1)} %reshape.345) | copy-start | bytes 1320964
  29.4 7.5 %copy-start.6 = (bf16[2,430,256]{2,1,0:T(8,128)(2,1)}, bf16[2,430,256]{2,1,0:T(8,128)(2,1)S(1)}, u32[]{:S(2)}) copy-start(bf16[2,430,256]{2,1,0:T(8,128)(2,1)S(1)} %reshape.348) | copy-start | bytes 1320964
  96.0 4.7 copy-start.29
  96.0 6.1 %copy-start.28 = (bf16[2,1024]{1,0:T(2,128)(2,1)S(1)}, bf16[2,1024]{1,0:T(2,128)(2,1)}, u32[]{:S(2)}) copy-start(bf16[2,1024]{1,0:T(2,128)(2,1)} %param.17) | copy-start | bytes 12292
  96.0 67.5 %all-to-all-start.1 = ((bf16[2,430,8,256]{3,0,1,2:T(2,128)(2,1)}), bf16[2,430,8,256]{3,0,1,2:T(2,128)(2,1)}, u32[]{:S(2)}, u32[]{:S(2)}) async-start(bf16[2,430,8,256]{3,0,1,2:T(2,128)(2,1)} %broadcast_in_dim.8), calls=%async_computation.1 | async-start | bytes 7045120 | tf_op jit(solution)/shard_map/all_to_all | solution.py:135
  100.6 370.3 %reduce-scatter.2.cloned.1.call-start = ((), (), s32[]{:S(2)}) async-start(), calls=%async_computation.3 | async-start | bytes 3981312 | tf_op jit(solution)/shard_map/reduce_scatter | solution.py:236
  100.7 39.3 %collective-permute-start = (bf16[256]{0:T(256)(128)(2,1)S(1)}, bf16[256]{0:T(256)(128)(2,1)S(1)}, u32[]{:S(2)}, u32[]{:S(2)}) collective-permute-start(bf16[256]{0:T(256)(128)(2,1)S(1)} %copy-done.29), channel_id=1, source_target_pairs={{0,1},{1,0},{2,3},{3,2},{4,5},{5,4},{6,7},{7,6},{8,9},{9,8},{10,11... | collective-permute-start | bytes 1544 | tf_op jit(solution)/shard_map/ppermute | solution.py:52
  102.1 3.3 collective-permute-start.6
  105.4 35.0 %collective-permute-start.7 = (bf16[4,1024]{1,0:T(4,128)(2,1)S(1)}, bf16[4,1024]{1,0:T(4,128)(2,1)S(1)}, u32[]{:S(2)}, u32[]{:S(2)}) collective-permute-start(bf16[4,1024]{1,0:T(4,128)(2,1)S(1)} %maximum_select_fusion.6), channel_id=1, source_target_pairs={{0,16},{8,24},{16,0},{24,8},{32,48},{40,56},{48,32},{56,40},{64,80... | collective-permute-start | bytes 24584 | tf_op jit(solution)/shard_map/ppermute | solution.py:52
  140.0 6.5 %collective-permute-start.1 = (bf16[512]{0:T(512)(128)(2,1)S(1)}, bf16[512]{0:T(512)(128)(2,1)S(1)}, u32[]{:S(2)}, u32[]{:S(2)}) collective-permute-start(bf16[512]{0:T(512)(128)(2,1)S(1)} %maximum_select_fusion.12), channel_id=1, source_target_pairs={{0,2},{1,3},{2,0},{3,1},{4,6},{5,7},{6,4},{7,5},{8,10},{9,11},{10,... | collective-permute-start | bytes 3080 | tf_op jit(solution)/shard_map/ppermute | solution.py:52
  140.4 17.4 %collective-permute-start.8 = (bf16[8,1024]{1,0:T(8,128)(2,1)S(1)}, bf16[8,1024]{1,0:T(8,128)(2,1)S(1)}, u32[]{:S(2)}, u32[]{:S(2)}) collective-permute-start(bf16[8,1024]{1,0:T(8,128)(2,1)S(1)} %maximum_select_fusion.3), channel_id=1, source_target_pairs={{0,32},{8,40},{16,48},{24,56},{32,0},{40,8},{48,16},{56,24},{64,96... | collective-permute-start | bytes 49160 | tf_op jit(solution)/shard_map/ppermute | solution.py:52
  146.5 12.8 %collective-permute-start.2 = (bf16[1024]{0:T(1024)(128)(2,1)S(1)}, bf16[1024]{0:T(1024)(128)(2,1)S(1)}, u32[]{:S(2)}, u32[]{:S(2)}) collective-permute-start(bf16[1024]{0:T(1024)(128)(2,1)S(1)} %maximum_select_fusion.11), channel_id=1, source_target_pairs={{0,4},{1,5},{2,6},{3,7},{4,0},{5,1},{6,2},{7,3},{8,12},{9,13},{10,... | collective-permute-start | bytes 6152 | tf_op jit(solution)/shard_map/ppermute | solution.py:52
  157.9 2.9 collective-permute-start.9
  160.7 28.4 %collective-permute-start.10 = (bf16[32,1024]{1,0:T(8,128)(2,1)S(1)}, bf16[32,1024]{1,0:T(8,128)(2,1)S(1)}, u32[]{:S(2)}, u32[]{:S(2)}) collective-permute-start(bf16[32,1024]{1,0:T(8,128)(2,1)S(1)} %maximum_select_fusion.1), channel_id=1, source_target_pairs={{0,128},{8,136},{16,144},{24,152},{32,160},{40,168},{48,176},{56,1... | collective-permute-start | bytes 196616 | tf_op jit(solution)/shard_map/ppermute | solution.py:52
  167.2 18.7 %copy-start.25 = (bf16[256,1024]{1,0:T(8,128)(2,1)S(1)}, bf16[256,1024]{1,0:T(8,128)(2,1)}, u32[]{:S(2)}) copy-start(bf16[256,1024]{1,0:T(8,128)(2,1)} %param.16) | copy-start | bytes 1572868
  186.1 2.5 collective-permute-start.3
  188.6 2.5 collective-permute-start.4
  191.1 4.0 collective-permute-start.5
  198.2 9.4 %collective-permute-start.11 = (f32[65]{0:T(128)S(1)}, f32[65]{0:T(128)S(1)}, u32[]{:S(2)}, u32[]{:S(2)}) collective-permute-start(f32[65]{0:T(128)S(1)} %pad_maximum_fusion.1), channel_id=1, source_target_pairs={{0,8},{8,0},{16,24},{24,16},{32,40},{40,32},{48,56},{56,48},{64,72... | collective-permute-start | bytes 788 | tf_op jit(solution)/shard_map/ppermute | solution.py:43
  207.7 3.3 collective-permute-start.12
  211.1 6.3 %collective-permute-start.13 = (f32[65]{0:T(128)S(1)}, f32[65]{0:T(128)S(1)}, u32[]{:S(2)}, u32[]{:S(2)}) collective-permute-start(f32[65]{0:T(128)S(1)} %add.237), channel_id=1, source_target_pairs={{0,32},{8,40},{16,48},{24,56},{32,0},{40,8},{48,16},{56,24},{64,96... | collective-permute-start | bytes 788 | tf_op jit(solution)/shard_map/ppermute | solution.py:43
  217.4 2.6 collective-permute-start.14
  220.0 3.9 collective-permute-start.15
  225.2 11.7 %collective-permute-start.16 = (f32[2,256]{1,0:T(2,128)S(1)}, f32[2,256]{1,0:T(2,128)S(1)}, u32[]{:S(2)}, u32[]{:S(2)}) collective-permute-start(f32[2,256]{1,0:T(2,128)S(1)} %fusion.134), channel_id=1, source_target_pairs={{0,1},{1,0},{2,3},{3,2},{4,5},{5,4},{6,7},{7,6},{8,9},{9,8},{10,11... | collective-permute-start | bytes 6152 | tf_op jit(solution)/shard_map/ppermute | solution.py:52
  236.9 8.2 %collective-permute-start.17 = (f32[2,512]{1,0:T(2,128)S(1)}, f32[2,512]{1,0:T(2,128)S(1)}, u32[]{:S(2)}, u32[]{:S(2)}) collective-permute-start(f32[2,512]{1,0:T(2,128)S(1)} %maximum_select_fusion.9), channel_id=1, source_target_pairs={{0,2},{1,3},{2,0},{3,1},{4,6},{5,7},{6,4},{7,5},{8,10},{9,11},{10,... | collective-permute-start | bytes 12296 | tf_op jit(solution)/shard_map/ppermute | solution.py:52
  245.2 4.5 collective-permute-start.18
  269.4 5.2 %copy-start.19 = (bf16[2,430,2,128]{3,2,1,0:T(2,128)(2,1)S(1)}, bf16[2,430,2,128]{3,2,1,0:T(2,128)(2,1)}, u32[]{:S(2)}) copy-start(bf16[2,430,2,128]{3,2,1,0:T(2,128)(2,1)} %copy-done.18) | copy-start | bytes 1320964
  277.0 7.4 %copy-start.17 = (bf16[2,430,2,128]{3,2,1,0:T(2,128)(2,1)S(1)}, bf16[2,430,2,128]{3,2,1,0:T(2,128)(2,1)}, u32[]{:S(2)}) copy-start(bf16[2,430,2,128]{3,2,1,0:T(2,128)(2,1)} %copy-done.16) | copy-start | bytes 1320964
  301.1 4.4 copy-start.7
  314.0 3.6 copy-start.26
  317.3 29.2 %collective-permute-start.24 = (bf16[16,24576]{1,0:T(8,128)(2,1)}, bf16[16,24576]{1,0:T(8,128)(2,1)}, u32[]{:S(2)}, u32[]{:S(2)}) collective-permute-start(bf16[16,24576]{1,0:T(8,128)(2,1)} %dynamic-slice_bitcast_fusion.1), channel_id=1, source_target_pairs={{0,128},{8,136},{16,144},{24,152},{32,160},{40,168},{48,176},{56,1... | collective-permute-start | bytes 2359304 | tf_op jit(solution)/shard_map/ppermute | solution.py:77
  348.3 6.7 %collective-permute-start.25 = (bf16[8,24576]{1,0:T(8,128)(2,1)S(1)}, bf16[8,24576]{1,0:T(8,128)(2,1)S(1)}, u32[]{:S(2)}, u32[]{:S(2)}) collective-permute-start(bf16[8,24576]{1,0:T(8,128)(2,1)S(1)} %fusion.84), channel_id=1, source_target_pairs={{0,64},{8,72},{16,80},{24,88},{32,96},{40,104},{48,112},{56,120},{... | collective-permute-start | bytes 1179656 | tf_op jit(solution)/shard_map/ppermute | solution.py:77
  355.4 9.9 %collective-permute-start.26 = (bf16[4,24576]{1,0:T(4,128)(2,1)S(1)}, bf16[4,24576]{1,0:T(4,128)(2,1)S(1)}, u32[]{:S(2)}, u32[]{:S(2)}) collective-permute-start(bf16[4,24576]{1,0:T(4,128)(2,1)S(1)} %fusion.97), channel_id=1, source_target_pairs={{0,32},{8,40},{16,48},{24,56},{32,0},{40,8},{48,16},{56,24},{64,96... | collective-permute-start | bytes 589832 | tf_op jit(solution)/shard_map/ppermute | solution.py:77
  360.8 29.6 %collective-permute-start.19 = (bf16[16,49152]{1,0:T(8,128)(2,1)}, bf16[16,49152]{1,0:T(8,128)(2,1)S(1)}, u32[]{:S(2)}, u32[]{:S(2)}) collective-permute-start(bf16[16,49152]{1,0:T(8,128)(2,1)} %dynamic-slice_bitcast_fusion), channel_id=1, source_target_pairs={{0,128},{8,136},{16,144},{24,152},{32,160},{40,168},{48,176},{56,1... | collective-permute-start | bytes 4718600 | tf_op jit(solution)/shard_map/ppermute | solution.py:77
  365.8 27.2 %collective-permute-start.27 = (bf16[2,24576]{1,0:T(2,128)(2,1)S(1)}, bf16[2,24576]{1,0:T(2,128)(2,1)S(1)}, u32[]{:S(2)}, u32[]{:S(2)}) collective-permute-start(bf16[2,24576]{1,0:T(2,128)(2,1)S(1)} %fusion.100), channel_id=1, source_target_pairs={{0,16},{8,24},{16,0},{24,8},{32,48},{40,56},{48,32},{56,40},{64,80... | collective-permute-start | bytes 294920 | tf_op jit(solution)/shard_map/ppermute | solution.py:77
  392.2 14.7 %collective-permute-start.20 = (bf16[8,49152]{1,0:T(8,128)(2,1)S(1)}, bf16[8,49152]{1,0:T(8,128)(2,1)S(1)}, u32[]{:S(2)}, u32[]{:S(2)}) collective-permute-start(bf16[8,49152]{1,0:T(8,128)(2,1)S(1)} %fusion.82), channel_id=1, source_target_pairs={{0,64},{8,72},{16,80},{24,88},{32,96},{40,104},{48,112},{56,120},{... | collective-permute-start | bytes 2359304 | tf_op jit(solution)/shard_map/ppermute | solution.py:77
  409.9 26.5 %collective-permute-start.21 = (bf16[4,49152]{1,0:T(4,128)(2,1)S(1)}, bf16[4,49152]{1,0:T(4,128)(2,1)S(1)}, u32[]{:S(2)}, u32[]{:S(2)}) collective-permute-start(bf16[4,49152]{1,0:T(4,128)(2,1)S(1)} %fusion.83), channel_id=1, source_target_pairs={{0,32},{8,40},{16,48},{24,56},{32,0},{40,8},{48,16},{56,24},{64,96... | collective-permute-start | bytes 1179656 | tf_op jit(solution)/shard_map/ppermute | solution.py:77
  413.4 27.5 %collective-permute-start.28 = (bf16[1,24576]{1,0:T(2,128)(2,1)S(1)}, bf16[1,24576]{1,0:T(2,128)(2,1)S(1)}, u32[]{:S(2)}, u32[]{:S(2)}) collective-permute-start(bf16[1,24576]{1,0:T(2,128)(2,1)S(1)} %dynamic-slice_convert_fusion.7), channel_id=1, source_target_pairs={{0,8},{8,0},{16,24},{24,16},{32,40},{40,32},{48,56},{56,48},{64,72... | collective-permute-start | bytes 147464 | tf_op jit(solution)/shard_map/ppermute | solution.py:77
  436.4 36.7 %copy-start.1 = (bf16[256,2048]{1,0:T(8,128)(2,1)S(1)}, bf16[256,2048]{1,0:T(8,128)(2,1)}, u32[]{:S(2)}) copy-start(bf16[256,2048]{1,0:T(8,128)(2,1)} %param.14) | copy-start | bytes 3145732
  438.6 10.5 %collective-permute-start.22 = (bf16[2,49152]{1,0:T(2,128)(2,1)S(1)}, bf16[2,49152]{1,0:T(2,128)(2,1)S(1)}, u32[]{:S(2)}, u32[]{:S(2)}) collective-permute-start(bf16[2,49152]{1,0:T(2,128)(2,1)S(1)} %fusion.96), channel_id=1, source_target_pairs={{0,16},{8,24},{16,0},{24,8},{32,48},{40,56},{48,32},{56,40},{64,80... | collective-permute-start | bytes 589832 | tf_op jit(solution)/shard_map/ppermute | solution.py:77
  449.5 11.4 %collective-permute-start.23 = (bf16[1,49152]{1,0:T(2,128)(2,1)S(1)}, bf16[1,49152]{1,0:T(2,128)(2,1)S(1)}, u32[]{:S(2)}, u32[]{:S(2)}) collective-permute-start(bf16[1,49152]{1,0:T(2,128)(2,1)S(1)} %dynamic-slice_convert_fusion.6), channel_id=1, source_target_pairs={{0,8},{8,0},{16,24},{24,16},{32,40},{40,32},{48,56},{56,48},{64,72... | collective-permute-start | bytes 294920 | tf_op jit(solution)/shard_map/ppermute | solution.py:77
  (13 other events, 23.6 us)
Sparse Core Ops, SparseCore 0:
  363.0 107.8 reduce-scatter.1
